TPU v7x, 512 devices: a whole 4x4x16 slice. The times are simulated.
512 devices in a mesh: ctx: 16 (over z), ep: 32 (over y, x, core).
Axes of the slice: x: 4, y: 4, z: 16, core: 2. Of those that a mesh axis runs over, the one named last changes fastest.
Arguments:
- query_act: bfloat16 [2048, 8192], P('ctx', 'ep'), may hold values from -6 to 6
- key_act: bfloat16 [2048, 8192], P('ctx', 'ep'), may hold values from -6 to 6
- value_act: bfloat16 [2048, 8192], P('ctx', 'ep'), may hold values from -6 to 6
- state_init: float32 [64, 128, 128], P('ep'), may hold values from -128 to 128
- head_gain: float32 [8192], P('ep'), may hold values from 0.25 to 1.75
- out_weight: bfloat16 [8192, 3072], P('ctx', 'ep'), may hold values from -0.0625 to 0.0625
- stream_in: bfloat16 [2048, 3072], P('ctx', 'ep'), may hold values from -150 to 150
- model_gain: float32 [3072], replicated, may hold values from 0.25 to 1.75
- expert_ids: int32 [2048, 2], P('ctx'), may hold values from 0 to 15, as said below
- expert_slots: int32 [2048, 2], P('ctx'), may hold values from 0 to 19, as said below
- route_gates: float32 [2048, 2], P('ctx'), may hold values from 0.2 to 1
- gate_weight: bfloat16 [32, 3072, 3072], P('ep', 'ctx'), may hold values from -0.109375 to 0.109375
- up_weight: bfloat16 [32, 3072, 3072], P('ep', 'ctx'), may hold values from -0.109375 to 0.109375
- down_weight: bfloat16 [32, 3072, 3072], P('ep', 'ctx'), may hold values from -0.078125 to 0.078125
- out_grad: bfloat16 [2048, 3072], P('ctx', 'ep'), may hold values from -6 to 6
Outputs:
- layer_out: bfloat16 [2048, 3072], P('ctx', 'ep')
- grad_query: bfloat16 [2048, 8192], P('ctx', 'ep')
- grad_key: bfloat16 [2048, 8192], P('ctx', 'ep')
- grad_value: bfloat16 [2048, 8192], P('ctx', 'ep')
- grad_state: float32 [64, 128, 128], P('ep')
- grad_stream: bfloat16 [2048, 3072], P('ctx', 'ep')
Inputs may be any that keep to these rules, and one draw needn't show every extreme that they name: `expert_ids`: within each block of 128 tokens a token's two experts differ; the tokens naming expert e hold the slots 0 to n - 1 of e once each, n being their number; no expert is named by more than 20 tokens of a block, and in every block some expert by exactly 20. `expert_slots`: see expert_ids.
All inputs are finite; a program needn't handle non-finite values.
Results may differ from a plain program's by a relative error of at most 0.02.
Values may be sent and summed in bfloat16 or wider, within the bound.
No kernel may reach another device: no remote copies, remote signals or barrier semaphores. Data moves between devices by JAX's collectives and lax.ppermute only.
A program may use at most 64 MiB of HBM per device.

v0:
```python
import jax
import jax.numpy as jnp
from jax import lax
from jax.sharding import PartitionSpec as P


def butterfly_sums(value, axis, backward):
    count = lax.axis_size(axis)
    place = lax.axis_index(axis)
    total = value
    carried = jnp.zeros_like(value)
    step = 1
    while step < count:
        other = lax.ppermute(total, axis, [(i, i ^ step) for i in range(count)])
        upper = place & step != 0
        take = jnp.logical_not(upper) if backward else upper
        carried = carried + jnp.where(take, other, jnp.zeros_like(other))
        total = total + other
        step *= 2
    return (carried, total)


def gather_blocks(value, axis):
    count = lax.axis_size(axis)
    spread = jnp.broadcast_to(value[None], (count,) + value.shape)
    return lax.all_to_all(spread, axis, 0, 0, tiled=True)


def scatter_sum(values, axis):
    count = lax.axis_size(axis)
    rows, width = values[0].shape
    block = rows // count
    joined = jnp.concatenate([value.reshape(count, block, width) for value in values], 1)
    part = lax.psum_scatter(joined, axis, scatter_dimension=0, tiled=True)
    return [part[0, i * block : (i + 1) * block] for i in range(len(values))]


def head_normalize(attended, gain):
    factor = lax.rsqrt(jnp.mean(attended * attended, -1, keepdims=True) + 1e-06)
    return attended * factor * gain


def contract_last(left, right):
    return lax.dot_general(
        left, right, (((1,), (1,)), ((), ())), preferred_element_type=jnp.float32
    )


def local(
    query_act,
    key_act,
    value_act,
    state_init,
    head_gain,
    out_weight,
    stream_in,
    model_gain,
    expert_ids,
    expert_slots,
    route_gates,
    gate_weight,
    up_weight,
    down_weight,
    out_grad,
):
    f32 = jnp.float32
    high = lax.Precision.HIGHEST
    ep_count = lax.axis_size("ep")
    expert_count = ep_count // 2
    my_ep = lax.axis_index("ep")
    tokens_here = query_act.shape[0]
    head_count = state_init.shape[0]
    head_size = state_init.shape[1]
    model_width = model_gain.shape[0]
    columns = stream_in.shape[1]
    capacity = 5 * tokens_here // (2 * expert_count)
    w_cols = lax.all_gather(out_weight, "ctx", axis=0, tiled=True)
    query3 = query_act.reshape(tokens_here, head_count, head_size)
    key3 = key_act.reshape(tokens_here, head_count, head_size)
    value3 = value_act.reshape(tokens_here, head_count, head_size)
    kv_own = jnp.einsum("thd,the->hde", key3, value3, preferred_element_type=f32)
    before, _ = butterfly_sums(kv_own, "ctx", False)
    prefix = state_init + before
    causal = jnp.arange(tokens_here)[:, None] >= jnp.arange(tokens_here)[None, :]
    scores = jnp.einsum("thd,shd->hts", query3, key3, preferred_element_type=f32)
    scores_bf = jnp.where(causal[None], scores, 0.0).astype(jnp.bfloat16)
    inside = jnp.einsum("hts,she->the", scores_bf, value3, preferred_element_type=f32)
    from_state = jnp.einsum("thd,hde->the", query3.astype(f32), prefix, precision=high)
    attended = from_state + inside
    gain_heads = head_gain.reshape(head_count, head_size)
    normed_heads = (
        head_normalize(attended, gain_heads)
        .astype(jnp.bfloat16)
        .reshape(tokens_here, head_count * head_size)
    )
    w_blocks = w_cols.reshape(ep_count, head_count * head_size, columns)
    attn_proj = jnp.einsum(
        "ith,ihf->tf", gather_blocks(normed_heads, "ep"), w_blocks, preferred_element_type=f32
    )
    stream = (stream_in.astype(f32) + attn_proj).astype(jnp.bfloat16)
    stream_f = stream.astype(f32)
    gain_cols = lax.dynamic_slice_in_dim(model_gain, my_ep * columns, columns, 0)
    dest_expert = jnp.arange(ep_count) % expert_count
    slot_iota = jnp.arange(capacity)
    hits = (expert_ids[:, :, None, None] == dest_expert[None, None, :, None]) & (
        expert_slots[:, :, None, None] == slot_iota[None, None, None, :]
    )
    hits_f = hits.astype(f32)
    dest_picks = jnp.sum(hits_f, 1).reshape(tokens_here, ep_count * capacity)
    dest_weights = jnp.sum(hits_f * route_gates[:, :, None, None], 1).reshape(
        tokens_here, ep_count * capacity
    )
    picked = jnp.dot(dest_picks.T.astype(jnp.bfloat16), stream, preferred_element_type=f32).astype(
        jnp.bfloat16
    )
    arrived = lax.all_to_all(picked.reshape(ep_count, capacity, columns), "ep", 0, 0, tiled=True)
    slot_rows = arrived.transpose(1, 0, 2).reshape(capacity, model_width).astype(f32)
    slot_scale = lax.rsqrt(jnp.mean(slot_rows * slot_rows, -1, keepdims=True) + 1e-05)
    expert_in = (slot_rows * slot_scale * model_gain).astype(jnp.bfloat16)
    w_gate = gate_weight[0]
    w_up = up_weight[0]
    w_down = down_weight[0]
    hidden_block = w_gate.shape[0]
    w_rows = lax.all_to_all(w_blocks, "ep", 0, 0, tiled=True)
    portion = lax.all_gather(expert_in, "ctx", axis=0, tiled=True)
    square_sums = jnp.sum(gather_blocks(jnp.sum(stream_f * stream_f, -1, keepdims=True), "ep"), 0)
    row_scale = lax.rsqrt(square_sums / model_width + 1e-05)
    projected = jnp.concatenate([contract_last(portion, w_gate), contract_last(portion, w_up)], 1)
    pre_gate = projected[:, :hidden_block]
    pre_up = projected[:, hidden_block:]
    gate_sig = jax.nn.sigmoid(pre_gate)
    activated = (pre_gate * gate_sig * pre_up).astype(jnp.bfloat16)
    out_terms = jnp.dot(activated, w_down, preferred_element_type=f32).astype(jnp.bfloat16)
    grad_out = out_grad.astype(f32)
    grad_send = jnp.dot(dest_weights.T, grad_out, precision=high).astype(jnp.bfloat16)
    grad_in = lax.all_to_all(grad_send, "ep", split_axis=0, concat_axis=1, tiled=True)
    grad_rows_all = lax.all_gather(grad_in, "ctx", axis=0, tiled=True)
    portion, w_rows, square_sums, grad_rows_all = lax.optimization_barrier(
        (portion, w_rows, square_sums, grad_rows_all)
    )
    row_scale = lax.rsqrt(square_sums / model_width + 1e-05)
    grad_act = contract_last(grad_rows_all, w_down)
    grad_gate_pre = (grad_act * pre_up * gate_sig * (1.0 + pre_gate * (1.0 - gate_sig))).astype(
        jnp.bfloat16
    )
    grad_up_pre = (grad_act * pre_gate * gate_sig).astype(jnp.bfloat16)
    grad_terms = (
        jnp.dot(grad_gate_pre, w_gate, preferred_element_type=f32)
        + jnp.dot(grad_up_pre, w_up, preferred_element_type=f32)
    ).astype(jnp.bfloat16)
    half_out, grad_half = scatter_sum([out_terms, grad_terms], "ctx")
    slot_inner = jnp.sum(slot_rows * model_gain * grad_half.astype(f32), -1, keepdims=True)
    inner_hi = slot_inner.astype(jnp.bfloat16)
    inner_lo = (slot_inner - inner_hi.astype(f32)).astype(jnp.bfloat16)
    inner_pair = jnp.broadcast_to(
        jnp.concatenate([inner_hi, inner_lo], -1)[:, None, :], (capacity, ep_count, 2)
    )
    payload = jnp.concatenate([grad_half.reshape(capacity, ep_count, columns), inner_pair], -1)
    grad_back = lax.all_to_all(payload, "ep", split_axis=1, concat_axis=0, tiled=True)
    grad_back = grad_back.reshape(ep_count * capacity, columns + 2).astype(f32)
    grad_model_in = jnp.dot(dest_picks, grad_back[:, :columns], precision=high)
    scaled_grad = grad_model_in * gain_cols
    inner_sum = jnp.dot(
        dest_picks,
        grad_back[:, columns : columns + 1] + grad_back[:, columns + 1 :],
        precision=high,
    )
    grad_stream = (
        grad_out + row_scale * scaled_grad - stream_f * row_scale**3 * inner_sum / model_width
    ).astype(jnp.bfloat16)
    grad_heads = jnp.einsum(
        "itf,ihf->th", gather_blocks(grad_stream, "ep"), w_rows, preferred_element_type=f32
    )
    head_pull = jax.vjp(lambda value: head_normalize(value, gain_heads), attended)[1]
    grad_attended = head_pull(grad_heads.reshape(tokens_here, head_count, head_size))[0].astype(
        jnp.bfloat16
    )
    state_part = jnp.einsum("thd,the->hde", query3, grad_attended, preferred_element_type=f32)
    half_out, state_part = lax.optimization_barrier((half_out, state_part))
    returned = lax.all_to_all(half_out, "ep", split_axis=1, concat_axis=0, tiled=True)
    expert_mix = jnp.dot(dest_weights, returned.astype(f32), precision=high)
    layer_out = (stream_f + expert_mix).astype(jnp.bfloat16)
    later_sum, state_total = butterfly_sums(state_part, "ctx", True)
    grad_scores = jnp.einsum("the,she->hts", grad_attended, value3, preferred_element_type=f32)
    grad_masked = jnp.where(causal[None], grad_scores, 0.0).astype(jnp.bfloat16)
    grad_att_f = grad_attended.astype(f32)
    grad_query = jnp.einsum("the,hde->thd", grad_att_f, prefix, precision=high) + jnp.einsum(
        "hts,shd->thd", grad_masked, key3, preferred_element_type=f32
    )
    grad_key = jnp.einsum(
        "the,hde->thd", value3.astype(f32), later_sum, precision=high
    ) + jnp.einsum("hts,thd->shd", grad_masked, query3, preferred_element_type=f32)
    grad_value = jnp.einsum(
        "thd,hde->the", key3.astype(f32), later_sum, precision=high
    ) + jnp.einsum("hts,the->she", scores_bf, grad_attended, preferred_element_type=f32)
    flat_shape = (tokens_here, head_count * head_size)
    return (
        layer_out,
        grad_query.astype(jnp.bfloat16).reshape(flat_shape),
        grad_key.astype(jnp.bfloat16).reshape(flat_shape),
        grad_value.astype(jnp.bfloat16).reshape(flat_shape),
        state_total,
        grad_stream,
    )


def solution(mesh):
    return jax.shard_map(
        local,
        mesh=mesh,
        in_specs=(
            P("ctx", "ep"),
            P("ctx", "ep"),
            P("ctx", "ep"),
            P("ep", None, None),
            P("ep"),
            P("ctx", "ep"),
            P("ctx", "ep"),
            P(),
            P("ctx", None),
            P("ctx", None),
            P("ctx", None),
            P("ep", "ctx", None),
            P("ep", "ctx", None),
            P("ep", "ctx", None),
            P("ctx", "ep"),
        ),
        out_specs=(
            P("ctx", "ep"),
            P("ctx", "ep"),
            P("ctx", "ep"),
            P("ctx", "ep"),
            P("ep", None, None),
            P("ctx", "ep"),
        ),
        check_vma=False,
    )
```

profile of v0, /device:TPU:1, one launch (start us, length us, event | category | flops | bytes accessed | tf_op | source)
XLA Modules:
  0.0 460.4 jit_solution(4378941329821075117)
XLA Ops:
  9.9 4.4 collective-permute-start
  17.7 4.9 %collective-permute-start.1 = (f32[2,128,128]{2,1,0:T(8,128)S(1)}, f32[2,128,128]{2,1,0:T(8,128)S(1)}, u32[]{:S(2)}, u32[]{:S(2)}) collective-permute-start(f32[2,128,128]{2,1,0:T(8,128)S(1)} %add.116), channel_id=1, source_target_pairs={{0,64},{32,96},{64,0},{96,32},{128,192},{160,224},{192,128},{224,1... | collective-permute-start | bytes 393224 | tf_op jit(solution)/shard_map/ppermute | solution.py:14
  23.9 8.4 %all-to-all-start.4 = ((bf16[32,20,96]{2,1,0:T(8,128)(2,1)}), bf16[32,20,96]{2,1,0:T(8,128)(2,1)S(1)}, u32[]{:S(2)}, u32[]{:S(2)}) async-start(bf16[32,20,96]{2,1,0:T(8,128)(2,1)} %all_to_all.56), calls=%async_computation.4 | async-start | bytes 393216 | tf_op jit(solution)/shard_map/all_to_all | solution.py:136
  32.5 8.8 %collective-permute-start.2 = (f32[2,128,128]{2,1,0:T(8,128)S(1)}, f32[2,128,128]{2,1,0:T(8,128)S(1)}, u32[]{:S(2)}, u32[]{:S(2)}) collective-permute-start(f32[2,128,128]{2,1,0:T(8,128)S(1)} %add.118), channel_id=1, source_target_pairs={{0,128},{32,160},{64,192},{96,224},{128,0},{160,32},{192,64},{224,... | collective-permute-start | bytes 393224 | tf_op jit(solution)/shard_map/ppermute | solution.py:14
  41.6 14.2 %collective-permute-done.2 = f32[2,128,128]{2,1,0:T(8,128)S(1)} collective-permute-done((f32[2,128,128]{2,1,0:T(8,128)S(1)}, f32[2,128,128]{2,1,0:T(8,128)S(1)}, u32[]{:S(2)}, u32[]{:S(2)}) %collective-permute-start.2) | collective-permute-done | bytes 131104 | tf_op jit(solution)/shard_map/ppermute | solution.py:14
  55.8 11.5 %collective-permute-start.3 = (f32[2,128,128]{2,1,0:T(8,128)S(1)}, f32[2,128,128]{2,1,0:T(8,128)S(1)}, u32[]{:S(2)}, u32[]{:S(2)}) collective-permute-start(f32[2,128,128]{2,1,0:T(8,128)S(1)} %add.120), channel_id=1, source_target_pairs={{0,256},{32,288},{64,320},{96,352},{128,384},{160,416},{192,448},{... | collective-permute-start | bytes 393224 | tf_op jit(solution)/shard_map/ppermute | solution.py:14
  67.5 4.1 collective-permute-done.3
  74.5 14.6 %all-to-all-start = ((bf16[32,128,256]{2,1,0:T(8,128)(2,1)}), bf16[32,128,256]{2,1,0:T(8,128)(2,1)}, u32[]{:S(2)}, u32[]{:S(2)}) async-start(bf16[32,128,256]{2,1,0:T(8,128)(2,1)} %broadcast_in_dim.30), calls=%async_computation | async-start | bytes 4194304 | tf_op jit(solution)/shard_map/all_to_all | solution.py:26
  90.5 27.4 %all-to-all-done = bf16[32,128,256]{2,1,0:T(8,128)(2,1)} async-done(((bf16[32,128,256]{2,1,0:T(8,128)(2,1)}), bf16[32,128,256]{2,1,0:T(8,128)(2,1)}, u32[]{:S(2)}, u32[]{:S(2)}) %all-to-all-start) | async-done | bytes 2097184 | tf_op jit(solution)/shard_map/all_to_all | solution.py:26
  121.7 12.8 %all_to_all.75 = bf16[32,20,96]{2,1,0:T(8,128)(2,1)S(1)} all-to-all(bf16[32,20,96]{2,1,0:T(8,128)(2,1)S(1)} %reshape.174), channel_id=1, replica_groups=mesh['ctx'=16,'ep'=32] {'ep'}, dimensions={0} | all-to-all | bytes 245760 | tf_op jit(solution)/shard_map/all_to_all | solution.py:116
  140.5 3.8 all-to-all-start.3
  145.8 5.4 %all-to-all-done.3 = f32[32,128,1]{1,2,0:T(1,128)S(1)} async-done(((f32[32,128,1]{1,2,0:T(1,128)}), f32[32,128,1]{1,2,0:T(1,128)S(1)}, u32[]{:S(2)}, u32[]{:S(2)}) %all-to-all-start.3) | async-done | bytes 16416 | tf_op jit(solution)/shard_map/all_to_all | solution.py:26
  151.2 4.3 all-to-all-start.2
  155.8 8.7 %all-gather.10.cloned.1.call-done = bf16[16,20,3072]{2,1,0:T(8,128)(2,1)} async-done(((bf16[1,20,3072]{2,1,0:T(8,128)(2,1)}), bf16[16,20,3072]{2,1,0:T(8,128)(2,1)}) %all-gather.10.cloned.1.call-update) | async-done | bytes 1966096 | tf_op jit(solution)/shard_map/all_gather | solution.py:137
  164.5 4.0 reshape.188
  168.5 68.1 %all-gather.8.cloned.1.call-done = bf16[16,20,3072]{2,1,0:T(8,128)(2,1)} async-done(((bf16[1,20,3072]{2,1,0:T(8,128)(2,1)}), bf16[16,20,3072]{2,1,0:T(8,128)(2,1)}) %all-gather.8.cloned.1.call-update) | async-done | bytes 1966096 | tf_op jit(solution)/shard_map/all_gather | solution.py:125
  236.5 3.9 reshape.186
  240.5 3.4 fusion.5
  250.5 3.9 reshape.177
  256.5 5.2 %pad_maximum_fusion = bf16[16,40,3072]{2,1,0:T(8,128)(2,1)} fusion(bf16[16,20,3072]{2,1,0:T(8,128)(2,1)} %reshape.177, bf16[16,20,3072]{2,1,0:T(8,128)(2,1)} %reshape.175), kind=kLoop, calls=%fused_computation.3 | loop fusion | flops 7864320 | bytes 7864320 | tf_op jit(solution)/shard_map/concatenate | solution.py:33
  261.9 75.8 %reduce-scatter.2.cloned.1.call-done = bf16[1,40,3072]{2,1,0:T(8,128)(2,1)} async-done(((bf16[16,40,3072]{2,1,0:T(8,128)(2,1)}), bf16[1,40,3072]{2,1,0:T(8,128)(2,1)}) %reduce-scatter.2.cloned.1.call-update) | async-done | bytes 245776 | tf_op jit(solution)/shard_map/reduce_scatter | solution.py:34
  340.8 18.3 %all-to-all-start.5 = ((bf16[20,32,98]{2,0,1:T(8,128)(2,1)}), bf16[20,32,98]{2,0,1:T(8,128)(2,1)S(1)}, u32[]{:S(2)}, u32[]{:S(2)}) async-start(bf16[20,32,98]{2,0,1:T(8,128)(2,1)} %copy.203), calls=%async_computation.6 | async-start | bytes 393216 | tf_op jit(solution)/shard_map/all_to_all | solution.py:159
  359.1 8.2 %all-to-all-done.5 = bf16[20,32,98]{2,0,1:T(8,128)(2,1)S(1)} async-done(((bf16[20,32,98]{2,0,1:T(8,128)(2,1)}), bf16[20,32,98]{2,0,1:T(8,128)(2,1)S(1)}, u32[]{:S(2)}, u32[]{:S(2)}) %all-to-all-start.5) | async-done | bytes 125472 | tf_op jit(solution)/shard_map/all_to_all | solution.py:159
  371.1 3.8 all-to-all-start.6
  374.9 14.3 %all-to-all-done.6 = bf16[32,128,96]{1,2,0:T(8,128)(2,1)S(1)} async-done(((bf16[32,128,96]{1,2,0:T(8,128)(2,1)}), bf16[32,128,96]{1,2,0:T(8,128)(2,1)S(1)}, u32[]{:S(2)}, u32[]{:S(2)}) %all-to-all-start.6) | async-done | bytes 786464 | tf_op jit(solution)/shard_map/all_to_all | solution.py:26
  395.4 4.5 all-to-all-start.7
  399.9 4.3 collective-permute-start.5
  404.4 6.1 %collective-permute-done.5 = f32[2,128,128]{2,1,0:T(8,128)S(1)} collective-permute-done((f32[2,128,128]{2,1,0:T(8,128)S(1)}, f32[2,128,128]{2,1,0:T(8,128)S(1)}, u32[]{:S(2)}, u32[]{:S(2)}) %collective-permute-start.5) | collective-permute-done | bytes 131104 | tf_op jit(solution)/shard_map/ppermute | solution.py:14
  410.6 6.0 %collective-permute-start.6 = (f32[2,128,128]{2,1,0:T(8,128)S(1)}, f32[2,128,128]{2,1,0:T(8,128)S(1)}, u32[]{:S(2)}, u32[]{:S(2)}) collective-permute-start(f32[2,128,128]{2,1,0:T(8,128)S(1)} %add.140), channel_id=1, source_target_pairs={{0,128},{32,160},{64,192},{96,224},{128,0},{160,32},{192,64},{224,... | collective-permute-start | bytes 393224 | tf_op jit(solution)/shard_map/ppermute | solution.py:14
  416.8 11.7 %collective-permute-done.6 = f32[2,128,128]{2,1,0:T(8,128)S(1)} collective-permute-done((f32[2,128,128]{2,1,0:T(8,128)S(1)}, f32[2,128,128]{2,1,0:T(8,128)S(1)}, u32[]{:S(2)}, u32[]{:S(2)}) %collective-permute-start.6) | collective-permute-done | bytes 131104 | tf_op jit(solution)/shard_map/ppermute | solution.py:14
  428.5 8.4 %collective-permute-start.7 = (f32[2,128,128]{2,1,0:T(8,128)S(1)}, f32[2,128,128]{2,1,0:T(8,128)S(1)}, u32[]{:S(2)}, u32[]{:S(2)}) collective-permute-start(f32[2,128,128]{2,1,0:T(8,128)S(1)} %add.142), channel_id=1, source_target_pairs={{0,256},{32,288},{64,320},{96,352},{128,384},{160,416},{192,448},{... | collective-permute-start | bytes 393224 | tf_op jit(solution)/shard_map/ppermute | solution.py:14
  438.0 13.2 %collective-permute-done.7 = f32[2,128,128]{2,1,0:T(8,128)S(1)} collective-permute-done((f32[2,128,128]{2,1,0:T(8,128)S(1)}, f32[2,128,128]{2,1,0:T(8,128)S(1)}, u32[]{:S(2)}, u32[]{:S(2)}) %collective-permute-start.7) | collective-permute-done | bytes 131104 | tf_op jit(solution)/shard_map/ppermute | solution.py:14
  (193 shorter events, 49.1 us)
Async XLA Ops:
  7.2 237.7 %copy-start = (bf16[1,192,3072]{2,1,0:T(8,128)(2,1)S(1)}, bf16[1,192,3072]{2,1,0:T(8,128)(2,1)}, u32[]{:S(2)}) copy-start(bf16[1,192,3072]{2,1,0:T(8,128)(2,1)} %param.28) | copy-start | bytes 3538948
  7.2 110.7 %all-gather.6.cloned.1.call-start = ((), (), s32[]{:S(2)}) async-start(), calls=%async_computation.9 | async-start | bytes 1671168 | tf_op jit(solution)/shard_map/all_gather | solution.py:77
  9.9 7.8 %collective-permute-start = (f32[2,128,128]{2,1,0:T(8,128)S(1)}, f32[2,128,128]{2,1,0:T(8,128)S(1)}, u32[]{:S(2)}, u32[]{:S(2)}) collective-permute-start(f32[2,128,128]{2,1,0:T(8,128)S(1)} %fusion.47), channel_id=1, source_target_pairs={{0,32},{32,0},{64,96},{96,64},{128,160},{160,128},{192,224},{224,1... | collective-permute-start | bytes 393224 | tf_op jit(solution)/shard_map/ppermute | solution.py:14
  17.6 49.7 %copy-start.23 = (bf16[128,256]{1,0:T(8,128)(2,1)S(1)}, bf16[128,256]{1,0:T(8,128)(2,1)}, u32[]{:S(2)}) copy-start(bf16[128,256]{1,0:T(8,128)(2,1)} %param.17) | copy-start | bytes 196612
  17.6 54.0 %copy-start.32 = (f32[2,128,128]{2,1,0:T(8,128)S(1)}, f32[2,128,128]{2,1,0:T(8,128)}, u32[]{:S(2)}) copy-start(f32[2,128,128]{2,1,0:T(8,128)} %param.18) | copy-start | bytes 393220
  17.7 14.8 %collective-permute-start.1 = (f32[2,128,128]{2,1,0:T(8,128)S(1)}, f32[2,128,128]{2,1,0:T(8,128)S(1)}, u32[]{:S(2)}, u32[]{:S(2)}) collective-permute-start(f32[2,128,128]{2,1,0:T(8,128)S(1)} %add.116), channel_id=1, source_target_pairs={{0,64},{32,96},{64,0},{96,32},{128,192},{160,224},{192,128},{224,1... | collective-permute-start | bytes 393224 | tf_op jit(solution)/shard_map/ppermute | solution.py:14
  23.0 49.7 %copy-start.37 = (f32[256]{0:T(256)S(1)}, f32[256]{0:T(256)}, u32[]{:S(2)}) copy-start(f32[256]{0:T(256)} %param.19) | copy-start | bytes 3076
  23.9 49.0 %all-to-all-start.4 = ((bf16[32,20,96]{2,1,0:T(8,128)(2,1)}), bf16[32,20,96]{2,1,0:T(8,128)(2,1)S(1)}, u32[]{:S(2)}, u32[]{:S(2)}) async-start(bf16[32,20,96]{2,1,0:T(8,128)(2,1)} %all_to_all.56), calls=%async_computation.4 | async-start | bytes 393216 | tf_op jit(solution)/shard_map/all_to_all | solution.py:136
  32.4 42.1 %copy-start.17 = (bf16[128,256]{0,1:T(8,128)(2,1)}, bf16[128,256]{0,1:T(8,128)(2,1)S(1)}, u32[]{:S(2)}) copy-start(bf16[128,256]{0,1:T(8,128)(2,1)S(1)} %copy.229) | copy-start | bytes 196612
  32.5 23.3 %collective-permute-start.2 = (f32[2,128,128]{2,1,0:T(8,128)S(1)}, f32[2,128,128]{2,1,0:T(8,128)S(1)}, u32[]{:S(2)}, u32[]{:S(2)}) collective-permute-start(f32[2,128,128]{2,1,0:T(8,128)S(1)} %add.118), channel_id=1, source_target_pairs={{0,128},{32,160},{64,192},{96,224},{128,0},{160,32},{192,64},{224,... | collective-permute-start | bytes 393224 | tf_op jit(solution)/shard_map/ppermute | solution.py:14
  41.6 33.0 %copy-start.28 = (bf16[2,128,128]{2,1,0:T(8,128)(2,1)}, bf16[2,128,128]{2,1,0:T(8,128)(2,1)S(1)}, u32[]{:S(2)}) copy-start(bf16[2,128,128]{2,1,0:T(8,128)(2,1)S(1)} %fusion.14) | copy-start | bytes 196612
  55.8 15.8 %collective-permute-start.3 = (f32[2,128,128]{2,1,0:T(8,128)S(1)}, f32[2,128,128]{2,1,0:T(8,128)S(1)}, u32[]{:S(2)}, u32[]{:S(2)}) collective-permute-start(f32[2,128,128]{2,1,0:T(8,128)S(1)} %add.120), channel_id=1, source_target_pairs={{0,256},{32,288},{64,320},{96,352},{128,384},{160,416},{192,448},{... | collective-permute-start | bytes 393224 | tf_op jit(solution)/shard_map/ppermute | solution.py:14
  74.5 43.4 %all-to-all-start = ((bf16[32,128,256]{2,1,0:T(8,128)(2,1)}), bf16[32,128,256]{2,1,0:T(8,128)(2,1)}, u32[]{:S(2)}, u32[]{:S(2)}) async-start(bf16[32,128,256]{2,1,0:T(8,128)(2,1)} %broadcast_in_dim.30), calls=%async_computation | async-start | bytes 4194304 | tf_op jit(solution)/shard_map/all_to_all | solution.py:26
  89.2 28.7 %copy-start.43 = (bf16[128,96]{0,1:T(8,128)(2,1)S(1)}, bf16[128,96]{0,1:T(8,128)(2,1)}, u32[]{:S(2)}) copy-start(bf16[128,96]{0,1:T(8,128)(2,1)} %param.21) | copy-start | bytes 73732
  89.2 75.3 %all-gather.10.cloned.1.call-start = ((), (), s32[]{:S(2)}) async-start(), calls=%async_computation.12 | async-start | bytes 2506752 | tf_op jit(solution)/shard_map/all_gather | solution.py:137
  90.2 146.4 %all-gather.8.cloned.1.call-start = ((), (), s32[]{:S(2)}) async-start(), calls=%async_computation.11 | async-start | bytes 2506752 | tf_op jit(solution)/shard_map/all_gather | solution.py:125
  121.3 247.5 %copy-start.30 = (bf16[128,96]{0,1:T(8,128)(2,1)}, bf16[128,96]{0,1:T(8,128)(2,1)S(1)}, u32[]{:S(2)}) copy-start(bf16[128,96]{0,1:T(8,128)(2,1)S(1)} %get-tuple-element.63) | copy-start | bytes 73732
  140.5 10.7 %all-to-all-start.3 = ((f32[32,128,1]{1,2,0:T(1,128)}), f32[32,128,1]{1,2,0:T(1,128)S(1)}, u32[]{:S(2)}, u32[]{:S(2)}) async-start(f32[32,128,1]{1,2,0:T(1,128)} %broadcast_in_dim.31), calls=%async_computation.3 | async-start | bytes 32768 | tf_op jit(solution)/shard_map/all_to_all | solution.py:26
  151.2 89.2 %all-to-all-start.2 = ((bf16[32,256,96]{1,2,0:T(8,128)(2,1)}), bf16[32,256,96]{1,2,0:T(8,128)(2,1)S(1)}, u32[]{:S(2)}, u32[]{:S(2)}) async-start(bf16[32,256,96]{1,2,0:T(8,128)(2,1)} %bitcast.172), calls=%async_computation.2 | async-start | bytes 3145728 | tf_op jit(solution)/shard_map/all_to_all | solution.py:124
  155.5 182.2 %reduce-scatter.2.cloned.1.call-start = ((), (), s32[]{:S(2)}) async-start(), calls=%async_computation.10 | async-start | bytes 4177920 | tf_op jit(solution)/shard_map/reduce_scatter | solution.py:34
  261.8 77.8 %copy-start.4 = (bf16[32,20,96]{2,1,0:T(8,128)(2,1)S(1)}, bf16[32,20,96]{2,1,0:T(8,128)(2,1)}, u32[]{:S(2)}) copy-start(bf16[32,20,96]{2,1,0:T(8,128)(2,1)} %copy-done.3) | copy-start | bytes 368644
  340.8 26.6 %all-to-all-start.5 = ((bf16[20,32,98]{2,0,1:T(8,128)(2,1)}), bf16[20,32,98]{2,0,1:T(8,128)(2,1)S(1)}, u32[]{:S(2)}, u32[]{:S(2)}) async-start(bf16[20,32,98]{2,0,1:T(8,128)(2,1)} %copy.203), calls=%async_computation.6 | async-start | bytes 393216 | tf_op jit(solution)/shard_map/all_to_all | solution.py:159
  371.1 18.1 %all-to-all-start.6 = ((bf16[32,128,96]{1,2,0:T(8,128)(2,1)}), bf16[32,128,96]{1,2,0:T(8,128)(2,1)S(1)}, u32[]{:S(2)}, u32[]{:S(2)}) async-start(bf16[32,128,96]{1,2,0:T(8,128)(2,1)} %broadcast_in_dim.33), calls=%async_computation.7 | async-start | bytes 1572864 | tf_op jit(solution)/shard_map/all_to_all | solution.py:26
  390.3 46.7 %copy-start.6 = (f32[128,32,20]{0,1,2:T(8,128)S(1)}, f32[128,32,20]{0,1,2:T(8,128)}, u32[]{:S(2)}) copy-start(f32[128,32,20]{0,1,2:T(8,128)} %copy-done.5) | copy-start | bytes 983044
  390.3 46.7 %copy-start.31 = (bf16[128,96]{0,1:T(8,128)(2,1)S(1)}, bf16[128,96]{0,1:T(8,128)(2,1)}, u32[]{:S(2)}) copy-start(bf16[128,96]{0,1:T(8,128)(2,1)} %copy-done.30) | copy-start | bytes 73732
  390.7 9.1 %collective-permute-start.4 = (f32[2,128,128]{2,1,0:T(8,128)S(1)}, f32[2,128,128]{2,1,0:T(8,128)S(1)}, u32[]{:S(2)}, u32[]{:S(2)}) collective-permute-start(f32[2,128,128]{2,1,0:T(8,128)S(1)} %convolution_bitcast_fusion.4), channel_id=1, source_target_pairs={{0,32},{32,0},{64,96},{96,64},{128,160},{160,128},{192,224},{224,1... | collective-permute-start | bytes 393224 | tf_op jit(solution)/shard_map/ppermute | solution.py:14
  394.7 57.2 %copy-start.27 = (bf16[128,256]{1,0:T(8,128)(2,1)S(1)}, bf16[128,256]{1,0:T(8,128)(2,1)}, u32[]{:S(2)}) copy-start(bf16[128,256]{1,0:T(8,128)(2,1)} %param.16) | copy-start | bytes 196612
  395.4 57.5 %copy-start.25 = (bf16[128,256]{1,0:T(8,128)(2,1)S(1)}, bf16[128,256]{1,0:T(8,128)(2,1)}, u32[]{:S(2)}) copy-start(bf16[128,256]{1,0:T(8,128)(2,1)} %param.17) | copy-start | bytes 196612
  395.4 41.6 %all-to-all-start.7 = ((bf16[20,32,96]{2,0,1:T(8,128)(2,1)}), bf16[20,32,96]{2,0,1:T(8,128)(2,1)S(1)}, u32[]{:S(2)}, u32[]{:S(2)}) async-start(bf16[20,32,96]{2,0,1:T(8,128)(2,1)} %copy.207), calls=%async_computation.8 | async-start | bytes 393216 | tf_op jit(solution)/shard_map/all_to_all | solution.py:180
  399.9 10.6 %collective-permute-start.5 = (f32[2,128,128]{2,1,0:T(8,128)S(1)}, f32[2,128,128]{2,1,0:T(8,128)S(1)}, u32[]{:S(2)}, u32[]{:S(2)}) collective-permute-start(f32[2,128,128]{2,1,0:T(8,128)S(1)} %add.138), channel_id=1, source_target_pairs={{0,64},{32,96},{64,0},{96,32},{128,192},{160,224},{192,128},{224,1... | collective-permute-start | bytes 393224 | tf_op jit(solution)/shard_map/ppermute | solution.py:14
  410.6 17.9 %collective-permute-start.6 = (f32[2,128,128]{2,1,0:T(8,128)S(1)}, f32[2,128,128]{2,1,0:T(8,128)S(1)}, u32[]{:S(2)}, u32[]{:S(2)}) collective-permute-start(f32[2,128,128]{2,1,0:T(8,128)S(1)} %add.140), channel_id=1, source_target_pairs={{0,128},{32,160},{64,192},{96,224},{128,0},{160,32},{192,64},{224,... | collective-permute-start | bytes 393224 | tf_op jit(solution)/shard_map/ppermute | solution.py:14
  428.5 22.6 %collective-permute-start.7 = (f32[2,128,128]{2,1,0:T(8,128)S(1)}, f32[2,128,128]{2,1,0:T(8,128)S(1)}, u32[]{:S(2)}, u32[]{:S(2)}) collective-permute-start(f32[2,128,128]{2,1,0:T(8,128)S(1)} %add.142), channel_id=1, source_target_pairs={{0,256},{32,288},{64,320},{96,352},{128,384},{160,416},{192,448},{... | collective-permute-start | bytes 393224 | tf_op jit(solution)/shard_map/ppermute | solution.py:14
  (31 other events, 219.2 us)
Sparse Core Ops, SparseCore 0:
  10.1 84.8 all-gather.5
  97.1 67.3 all-gather.9
  166.6 69.8 all-gather.7
  261.9 75.7 reduce-scatter.1
where the time goes:
time: 462 us; the launch traced here: 460 us
  waiting for transfers between devices  258 us (56%)
  starting transfers between devices  109 us (24%)
  local copies, waits for them, and re-layouts  35.1 us (8%)
  matrix products  19.3 us (4%)
  between operations  14.7 us (3%)
  blocking collectives  12.8 us (3%)
  other arithmetic  11.5 us (2%)
    reduce_scatter x1, waiting for transfers between devices, scatter_sum(): part = lax.psum_scatter(joined, axis, scatter_dimension=0, tiled=True)  75.8 us
    all_gather x1, waiting for transfers between devices, local(): portion = lax.all_gather(expert_in, 'ctx', axis=0, tiled=True)  68.1 us
    ppermute x8, starting transfers between devices, butterfly_sums(): other = lax.ppermute(total, axis, [(i, i ^ step) for i in range(count)])  50.9 us
    ppermute x8, waiting for transfers between devices, butterfly_sums(): other = lax.ppermute(total, axis, [(i, i ^ step) for i in range(count)])  49.4 us
    all_to_all x3, waiting for transfers between devices, gather_blocks(): return lax.all_to_all(spread, axis, 0, 0, tiled=True)  47.1 us
    all_to_all x3, starting transfers between devices, gather_blocks(): return lax.all_to_all(spread, axis, 0, 0, tiled=True)  22.2 us
    all_to_all x1, starting transfers between devices, local(): lax.all_to_all(payload, 'ep', split_axis=1, concat_axis=0, tiled=True)  18.3 us
    all_to_all x1, blocking collectives, local(): lax.all_to_all(picked.reshape(ep_count, capacity, columns), 'ep', 0, 0, t...  12.8 us
  transfers between devices with their start and end apart: 19, of which 12 were waited for; matrix products, arithmetic and copies ran while one was open for 7% of the time, Pallas kernels for 0%

commit v1 on v0

--- a/solution.py
+++ b/solution.py
@@ -122,7 +122,10 @@
     w_down = down_weight[0]
     hidden_block = w_gate.shape[0]
     w_rows = lax.all_to_all(w_blocks, "ep", 0, 0, tiled=True)
-    portion = lax.all_gather(expert_in, "ctx", axis=0, tiled=True)
+    peers = lax.axis_size("ctx")
+    blocks = jnp.stack([expert_in for _ in range(peers)])
+    blocks = lax.all_to_all(blocks, "ctx", split_axis=0, concat_axis=0)
+    portion = jnp.concatenate(blocks, axis=0)
     square_sums = jnp.sum(gather_blocks(jnp.sum(stream_f * stream_f, -1, keepdims=True), "ep"), 0)
     row_scale = lax.rsqrt(square_sums / model_width + 1e-05)
     projected = jnp.concatenate([contract_last(portion, w_gate), contract_last(portion, w_up)], 1)

time: 462 us -> 528 us (1.14)
  waiting for transfers between devices: 258 us -> 332 us
  blocking collectives: 12.8 us -> 0 us
    all_to_all x0 -> x2, waiting for transfers between devices: none -> 122 us  [the longest x1 115 us: local(): blocks = lax.all_to_all(blocks, 'ctx', split_axis=0, concat_axis=0)]
    all_gather x1 -> x0, waiting for transfers between devices: 68.1 us -> none  [local(): portion = lax.all_gather(expert_in, 'ctx', axis=0, tiled=True)]
    ppermute x8, waiting for transfers between devices: 49.4 us -> 67.7 us  [butterfly_sums(): other = lax.ppermute(total, axis, [(i, i ^ step) for i in range(count)])]
    all_to_all x1 -> x0, blocking collectives: 12.8 us -> none  [local(): lax.all_to_all(picked.reshape(ep_count, capacity, columns), 'ep', 0, 0, t...]
    all_to_all x0 -> x2, starting transfers between devices: none -> 12.6 us  [the longest x1 7.33 us: local(): blocks = lax.all_to_all(blocks, 'ctx', split_axis=0, concat_axis=0)]
    reduce_scatter x1, waiting for transfers between devices: 75.8 us -> 64.7 us  [scatter_sum(): part = lax.psum_scatter(joined, axis, scatter_dimension=0, tiled=True)]
    all_to_all x1, waiting for transfers between devices: 0.01 us -> 7.73 us  [local(): lax.all_to_all(grad_send, 'ep', split_axis=0, concat_axis=1, tiled=True)]
    all_to_all x3, starting transfers between devices: 22.2 us -> 15.6 us  [gather_blocks(): return lax.all_to_all(spread, axis, 0, 0, tiled=True)]
  transfers between devices with their start and end apart: 19 -> 20, of which waited for: 12 -> 18; matrix products, arithmetic and copies ran while one was open for 7% -> 5% of each run, Pallas kernels for 0% -> 0%
where the time goes in v1:
time: 528 us; the launch traced here: 526 us
  waiting for transfers between devices  332 us (63%)
  starting transfers between devices  114 us (22%)
  local copies, waits for them, and re-layouts  35.9 us (7%)
  matrix products  21.3 us (4%)
  between operations  14.8 us (3%)
  other arithmetic  8.24 us (2%)
    all_to_all x1, waiting for transfers between devices, local(): blocks = lax.all_to_all(blocks, 'ctx', split_axis=0, concat_axis=0)  115 us
    ppermute x8, waiting for transfers between devices, butterfly_sums(): other = lax.ppermute(total, axis, [(i, i ^ step) for i in range(count)])  67.7 us
    reduce_scatter x1, waiting for transfers between devices, scatter_sum(): part = lax.psum_scatter(joined, axis, scatter_dimension=0, tiled=True)  64.7 us
    ppermute x8, starting transfers between devices, butterfly_sums(): other = lax.ppermute(total, axis, [(i, i ^ step) for i in range(count)])  53.3 us
    all_to_all x3, waiting for transfers between devices, gather_blocks(): return lax.all_to_all(spread, axis, 0, 0, tiled=True)  48.9 us
    all_to_all x1, starting transfers between devices, local(): lax.all_to_all(payload, 'ep', split_axis=1, concat_axis=0, tiled=True)  18.3 us
    all_to_all x3, starting transfers between devices, gather_blocks(): return lax.all_to_all(spread, axis, 0, 0, tiled=True)  15.6 us
  transfers between devices with their start and end apart: 20, of which 18 were waited for; matrix products, arithmetic and copies ran while one was open for 5% of the time, Pallas kernels for 0%

profile of v1, /device:TPU:1, one launch (start us, length us, event | category | flops | bytes accessed | tf_op | source)
XLA Modules:
  0.0 526.3 jit_solution(12627805411597208756)
XLA Ops:
  9.3 4.4 collective-permute-start
  16.1 5.6 %collective-permute-start.1 = (f32[2,128,128]{2,1,0:T(8,128)S(1)}, f32[2,128,128]{2,1,0:T(8,128)S(1)}, u32[]{:S(2)}, u32[]{:S(2)}) collective-permute-start(f32[2,128,128]{2,1,0:T(8,128)S(1)} %add.116), channel_id=1, source_target_pairs={{0,64},{32,96},{64,0},{96,32},{128,192},{160,224},{192,128},{224,1... | collective-permute-start | bytes 393224 | tf_op jit(solution)/shard_map/ppermute | solution.py:14
  25.5 10.8 %collective-permute-start.2 = (f32[2,128,128]{2,1,0:T(8,128)S(1)}, f32[2,128,128]{2,1,0:T(8,128)S(1)}, u32[]{:S(2)}, u32[]{:S(2)}) collective-permute-start(f32[2,128,128]{2,1,0:T(8,128)S(1)} %add.118), channel_id=1, source_target_pairs={{0,128},{32,160},{64,192},{96,224},{128,0},{160,32},{192,64},{224,... | collective-permute-start | bytes 393224 | tf_op jit(solution)/shard_map/ppermute | solution.py:14
  37.4 9.6 %collective-permute-done.2 = f32[2,128,128]{2,1,0:T(8,128)S(1)} collective-permute-done((f32[2,128,128]{2,1,0:T(8,128)S(1)}, f32[2,128,128]{2,1,0:T(8,128)S(1)}, u32[]{:S(2)}, u32[]{:S(2)}) %collective-permute-start.2) | collective-permute-done | bytes 131104 | tf_op jit(solution)/shard_map/ppermute | solution.py:14
  47.0 15.2 %collective-permute-start.3 = (f32[2,128,128]{2,1,0:T(8,128)S(1)}, f32[2,128,128]{2,1,0:T(8,128)S(1)}, u32[]{:S(2)}, u32[]{:S(2)}) collective-permute-start(f32[2,128,128]{2,1,0:T(8,128)S(1)} %add.120), channel_id=1, source_target_pairs={{0,256},{32,288},{64,320},{96,352},{128,384},{160,416},{192,448},{... | collective-permute-start | bytes 393224 | tf_op jit(solution)/shard_map/ppermute | solution.py:14
  62.5 14.7 %collective-permute-done.3 = f32[2,128,128]{2,1,0:T(8,128)S(1)} collective-permute-done((f32[2,128,128]{2,1,0:T(8,128)S(1)}, f32[2,128,128]{2,1,0:T(8,128)S(1)}, u32[]{:S(2)}, u32[]{:S(2)}) %collective-permute-start.3) | collective-permute-done | bytes 131104 | tf_op jit(solution)/shard_map/ppermute | solution.py:14
  80.1 7.8 %all-to-all-start = ((bf16[32,128,256]{2,1,0:T(8,128)(2,1)}), bf16[32,128,256]{2,1,0:T(8,128)(2,1)}, u32[]{:S(2)}, u32[]{:S(2)}) async-start(bf16[32,128,256]{2,1,0:T(8,128)(2,1)} %broadcast_in_dim.30), calls=%async_computation | async-start | bytes 4194304 | tf_op jit(solution)/shard_map/all_to_all | solution.py:26
  88.8 27.9 %all-to-all-done = bf16[32,128,256]{2,1,0:T(8,128)(2,1)} async-done(((bf16[32,128,256]{2,1,0:T(8,128)(2,1)}), bf16[32,128,256]{2,1,0:T(8,128)(2,1)}, u32[]{:S(2)}, u32[]{:S(2)}) %all-to-all-start) | async-done | bytes 2097184 | tf_op jit(solution)/shard_map/all_to_all | solution.py:26
  120.7 5.3 %all-to-all-start.1 = ((bf16[32,20,96]{2,1,0:T(8,128)(2,1)}), bf16[32,20,96]{2,1,0:T(8,128)(2,1)S(1)}, u32[]{:S(2)}, u32[]{:S(2)}) async-start(bf16[32,20,96]{2,1,0:T(8,128)(2,1)} %reshape.195), calls=%async_computation.1 | async-start | bytes 393216 | tf_op jit(solution)/shard_map/all_to_all | solution.py:116
  127.3 7.1 %all-to-all-done.1 = bf16[32,20,96]{2,1,0:T(8,128)(2,1)S(1)} async-done(((bf16[32,20,96]{2,1,0:T(8,128)(2,1)}), bf16[32,20,96]{2,1,0:T(8,128)(2,1)S(1)}, u32[]{:S(2)}, u32[]{:S(2)}) %all-to-all-start.1) | async-done | bytes 122912 | tf_op jit(solution)/shard_map/all_to_all | solution.py:116
  134.3 3.8 all-to-all-start.5
  138.7 7.7 %all-to-all-done.5 = bf16[32,20,96]{2,1,0:T(8,128)(2,1)S(1)} async-done(((bf16[32,20,96]{2,1,0:T(8,128)(2,1)}), bf16[32,20,96]{2,1,0:T(8,128)(2,1)S(1)}, u32[]{:S(2)}, u32[]{:S(2)}) %all-to-all-start.5) | async-done | bytes 122912 | tf_op jit(solution)/shard_map/all_to_all | solution.py:139
  151.0 6.8 %all-to-all-done.4 = f32[32,128,1]{1,2,0:T(1,128)S(1)} async-done(((f32[32,128,1]{1,2,0:T(1,128)}), f32[32,128,1]{1,2,0:T(1,128)S(1)}, u32[]{:S(2)}, u32[]{:S(2)}) %all-to-all-start.4) | async-done | bytes 16416 | tf_op jit(solution)/shard_map/all_to_all | solution.py:26
  159.5 7.3 %all-to-all-start.2 = ((bf16[16,20,3072]{2,1,0:T(8,128)(2,1)}), bf16[16,20,3072]{2,1,0:T(8,128)(2,1)S(1)}, u32[]{:S(2)}, u32[]{:S(2)}) async-start(bf16[16,20,3072]{2,1,0:T(8,128)(2,1)} %stack.2), calls=%async_computation.2 | async-start | bytes 4718592 | tf_op jit(solution)/shard_map/all_to_all | solution.py:127
  173.1 114.9 %all-to-all-done.2 = bf16[16,20,3072]{2,1,0:T(8,128)(2,1)S(1)} async-done(((bf16[16,20,3072]{2,1,0:T(8,128)(2,1)}), bf16[16,20,3072]{2,1,0:T(8,128)(2,1)S(1)}, u32[]{:S(2)}, u32[]{:S(2)}) %all-to-all-start.2) | async-done | bytes 1966112 | tf_op jit(solution)/shard_map/all_to_all | solution.py:127
  288.0 5.9 %all-to-all-start.3 = ((bf16[32,256,96]{1,2,0:T(8,128)(2,1)}), bf16[32,256,96]{1,2,0:T(8,128)(2,1)}, u32[]{:S(2)}, u32[]{:S(2)}) async-start(bf16[32,256,96]{1,2,0:T(8,128)(2,1)} %bitcast.170), calls=%async_computation.3 | async-start | bytes 3145728 | tf_op jit(solution)/shard_map/all_to_all | solution.py:124
  294.7 7.1 %all-gather.6.cloned.1.call-done = bf16[16,20,3072]{2,1,0:T(8,128)(2,1)} async-done(((bf16[1,20,3072]{2,1,0:T(8,128)(2,1)}), bf16[16,20,3072]{2,1,0:T(8,128)(2,1)}) %all-gather.6.cloned.1.call-update) | async-done | bytes 1966096 | tf_op jit(solution)/shard_map/all_gather | solution.py:140
  301.8 4.0 reshape.208
  310.6 5.8 %all-to-all-done.3 = bf16[32,256,96]{1,2,0:T(8,128)(2,1)} async-done(((bf16[32,256,96]{1,2,0:T(8,128)(2,1)}), bf16[32,256,96]{1,2,0:T(8,128)(2,1)}, u32[]{:S(2)}, u32[]{:S(2)}) %all-to-all-start.3) | async-done | bytes 1572896 | tf_op jit(solution)/shard_map/all_to_all | solution.py:124
  324.7 4.0 reshape.199
  330.8 5.2 pad_maximum_fusion
  336.9 64.7 %reduce-scatter.2.cloned.1.call-done = bf16[1,40,3072]{2,1,0:T(8,128)(2,1)} async-done(((bf16[16,40,3072]{2,1,0:T(8,128)(2,1)}), bf16[1,40,3072]{2,1,0:T(8,128)(2,1)}) %reduce-scatter.2.cloned.1.call-update) | async-done | bytes 245776 | tf_op jit(solution)/shard_map/reduce_scatter | solution.py:34
  404.1 18.3 %all-to-all-start.6 = ((bf16[20,32,98]{2,0,1:T(8,128)(2,1)}), bf16[20,32,98]{2,0,1:T(8,128)(2,1)S(1)}, u32[]{:S(2)}, u32[]{:S(2)}) async-start(bf16[20,32,98]{2,0,1:T(8,128)(2,1)} %copy.203), calls=%async_computation.7 | async-start | bytes 393216 | tf_op jit(solution)/shard_map/all_to_all | solution.py:162
  422.5 8.2 %all-to-all-done.6 = bf16[20,32,98]{2,0,1:T(8,128)(2,1)S(1)} async-done(((bf16[20,32,98]{2,0,1:T(8,128)(2,1)}), bf16[20,32,98]{2,0,1:T(8,128)(2,1)S(1)}, u32[]{:S(2)}, u32[]{:S(2)}) %all-to-all-start.6) | async-done | bytes 125472 | tf_op jit(solution)/shard_map/all_to_all | solution.py:162
  432.9 3.9 all-to-all-start.7
  436.9 14.2 %all-to-all-done.7 = bf16[32,128,96]{1,2,0:T(8,128)(2,1)S(1)} async-done(((bf16[32,128,96]{1,2,0:T(8,128)(2,1)}), bf16[32,128,96]{1,2,0:T(8,128)(2,1)S(1)}, u32[]{:S(2)}, u32[]{:S(2)}) %all-to-all-start.7) | async-done | bytes 786464 | tf_op jit(solution)/shard_map/all_to_all | solution.py:26
  454.9 4.0 all-to-all-start.8
  469.5 7.1 %collective-permute-done.5 = f32[2,128,128]{2,1,0:T(8,128)S(1)} collective-permute-done((f32[2,128,128]{2,1,0:T(8,128)S(1)}, f32[2,128,128]{2,1,0:T(8,128)S(1)}, u32[]{:S(2)}, u32[]{:S(2)}) %collective-permute-start.5) | collective-permute-done | bytes 131104 | tf_op jit(solution)/shard_map/ppermute | solution.py:14
  476.6 5.0 collective-permute-start.6
  481.7 13.5 %collective-permute-done.6 = f32[2,128,128]{2,1,0:T(8,128)S(1)} collective-permute-done((f32[2,128,128]{2,1,0:T(8,128)S(1)}, f32[2,128,128]{2,1,0:T(8,128)S(1)}, u32[]{:S(2)}, u32[]{:S(2)}) %collective-permute-start.6) | collective-permute-done | bytes 131104 | tf_op jit(solution)/shard_map/ppermute | solution.py:14
  495.2 6.3 %collective-permute-start.7 = (f32[2,128,128]{2,1,0:T(8,128)S(1)}, f32[2,128,128]{2,1,0:T(8,128)S(1)}, u32[]{:S(2)}, u32[]{:S(2)}) collective-permute-start(f32[2,128,128]{2,1,0:T(8,128)S(1)} %add.142), channel_id=1, source_target_pairs={{0,256},{32,288},{64,320},{96,352},{128,384},{160,416},{192,448},{... | collective-permute-start | bytes 393224 | tf_op jit(solution)/shard_map/ppermute | solution.py:14
  502.5 14.5 %collective-permute-done.7 = f32[2,128,128]{2,1,0:T(8,128)S(1)} collective-permute-done((f32[2,128,128]{2,1,0:T(8,128)S(1)}, f32[2,128,128]{2,1,0:T(8,128)S(1)}, u32[]{:S(2)}, u32[]{:S(2)}) %collective-permute-start.7) | collective-permute-done | bytes 131104 | tf_op jit(solution)/shard_map/ppermute | solution.py:14
  (196 shorter events, 70.7 us)
Async XLA Ops:
  7.2 312.0 %copy-start = (bf16[1,192,3072]{2,1,0:T(8,128)(2,1)S(1)}, bf16[1,192,3072]{2,1,0:T(8,128)(2,1)}, u32[]{:S(2)}) copy-start(bf16[1,192,3072]{2,1,0:T(8,128)(2,1)} %param.28) | copy-start | bytes 3538948
  7.2 55.1 %copy-start.19 = (bf16[128,256]{1,0:T(8,128)(2,1)S(1)}, bf16[128,256]{1,0:T(8,128)(2,1)}, u32[]{:S(2)}) copy-start(bf16[128,256]{1,0:T(8,128)(2,1)} %param.17) | copy-start | bytes 196612
  7.2 70.1 %copy-start.26 = (f32[2,128,128]{2,1,0:T(8,128)S(1)}, f32[2,128,128]{2,1,0:T(8,128)}, u32[]{:S(2)}) copy-start(f32[2,128,128]{2,1,0:T(8,128)} %param.18) | copy-start | bytes 393220
  7.2 71.1 %copy-start.34 = (f32[256]{0:T(256)S(1)}, f32[256]{0:T(256)}, u32[]{:S(2)}) copy-start(f32[256]{0:T(256)} %param.19) | copy-start | bytes 3076
  7.2 109.5 %all-gather.4.cloned.1.call-start = ((), (), s32[]{:S(2)}) async-start(), calls=%async_computation.10 | async-start | bytes 1671168 | tf_op jit(solution)/shard_map/all_gather | solution.py:77
  9.3 6.7 %collective-permute-start = (f32[2,128,128]{2,1,0:T(8,128)S(1)}, f32[2,128,128]{2,1,0:T(8,128)S(1)}, u32[]{:S(2)}, u32[]{:S(2)}) collective-permute-start(f32[2,128,128]{2,1,0:T(8,128)S(1)} %fusion.46), channel_id=1, source_target_pairs={{0,32},{32,0},{64,96},{96,64},{128,160},{160,128},{192,224},{224,1... | collective-permute-start | bytes 393224 | tf_op jit(solution)/shard_map/ppermute | solution.py:14
  16.1 9.4 %collective-permute-start.1 = (f32[2,128,128]{2,1,0:T(8,128)S(1)}, f32[2,128,128]{2,1,0:T(8,128)S(1)}, u32[]{:S(2)}, u32[]{:S(2)}) collective-permute-start(f32[2,128,128]{2,1,0:T(8,128)S(1)} %add.116), channel_id=1, source_target_pairs={{0,64},{32,96},{64,0},{96,32},{128,192},{160,224},{192,128},{224,1... | collective-permute-start | bytes 393224 | tf_op jit(solution)/shard_map/ppermute | solution.py:14
  22.7 57.4 %copy-start.14 = (bf16[128,256]{0,1:T(8,128)(2,1)}, bf16[128,256]{0,1:T(8,128)(2,1)S(1)}, u32[]{:S(2)}) copy-start(bf16[128,256]{0,1:T(8,128)(2,1)S(1)} %copy.229) | copy-start | bytes 196612
  22.8 39.8 %copy-start.32 = (pred[128,128]{1,0:T(8,128)(4,1)}, pred[128,128]{1,0:T(8,128)(4,1)S(1)}, u32[]{:S(2)}) copy-start(pred[128,128]{1,0:T(8,128)(4,1)S(1)} %iota_compare_fusion) | copy-start | bytes 49156
  25.5 21.5 %collective-permute-start.2 = (f32[2,128,128]{2,1,0:T(8,128)S(1)}, f32[2,128,128]{2,1,0:T(8,128)S(1)}, u32[]{:S(2)}, u32[]{:S(2)}) collective-permute-start(f32[2,128,128]{2,1,0:T(8,128)S(1)} %add.118), channel_id=1, source_target_pairs={{0,128},{32,160},{64,192},{96,224},{128,0},{160,32},{192,64},{224,... | collective-permute-start | bytes 393224 | tf_op jit(solution)/shard_map/ppermute | solution.py:14
  47.0 30.2 %collective-permute-start.3 = (f32[2,128,128]{2,1,0:T(8,128)S(1)}, f32[2,128,128]{2,1,0:T(8,128)S(1)}, u32[]{:S(2)}, u32[]{:S(2)}) collective-permute-start(f32[2,128,128]{2,1,0:T(8,128)S(1)} %add.120), channel_id=1, source_target_pairs={{0,256},{32,288},{64,320},{96,352},{128,384},{160,416},{192,448},{... | collective-permute-start | bytes 393224 | tf_op jit(solution)/shard_map/ppermute | solution.py:14
  80.1 36.6 %all-to-all-start = ((bf16[32,128,256]{2,1,0:T(8,128)(2,1)}), bf16[32,128,256]{2,1,0:T(8,128)(2,1)}, u32[]{:S(2)}, u32[]{:S(2)}) async-start(bf16[32,128,256]{2,1,0:T(8,128)(2,1)} %broadcast_in_dim.30), calls=%async_computation | async-start | bytes 4194304 | tf_op jit(solution)/shard_map/all_to_all | solution.py:26
  88.3 31.3 %copy-start.5 = (f32[128,32,20]{0,1,2:T(8,128)}, f32[128,32,20]{0,1,2:T(8,128)S(1)}, u32[]{:S(2)}) copy-start(f32[128,32,20]{0,1,2:T(8,128)S(1)} %get-tuple-element.53) | copy-start | bytes 983044
  88.5 31.1 %copy-start.1 = (f32[128,640]{0,1:T(8,128)}, f32[128,640]{0,1:T(8,128)S(1)}, u32[]{:S(2)}) copy-start(f32[128,640]{0,1:T(8,128)S(1)} %reshape.194) | copy-start | bytes 983044
  120.7 13.6 %all-to-all-start.1 = ((bf16[32,20,96]{2,1,0:T(8,128)(2,1)}), bf16[32,20,96]{2,1,0:T(8,128)(2,1)S(1)}, u32[]{:S(2)}, u32[]{:S(2)}) async-start(bf16[32,20,96]{2,1,0:T(8,128)(2,1)} %reshape.195), calls=%async_computation.1 | async-start | bytes 393216 | tf_op jit(solution)/shard_map/all_to_all | solution.py:116
  134.3 12.1 %all-to-all-start.5 = ((bf16[32,20,96]{2,1,0:T(8,128)(2,1)}), bf16[32,20,96]{2,1,0:T(8,128)(2,1)S(1)}, u32[]{:S(2)}, u32[]{:S(2)}) async-start(bf16[32,20,96]{2,1,0:T(8,128)(2,1)} %all_to_all.60), calls=%async_computation.5 | async-start | bytes 393216 | tf_op jit(solution)/shard_map/all_to_all | solution.py:139
  147.1 10.7 %all-to-all-start.4 = ((f32[32,128,1]{1,2,0:T(1,128)}), f32[32,128,1]{1,2,0:T(1,128)S(1)}, u32[]{:S(2)}, u32[]{:S(2)}) async-start(f32[32,128,1]{1,2,0:T(1,128)} %broadcast_in_dim.31), calls=%async_computation.4 | async-start | bytes 32768 | tf_op jit(solution)/shard_map/all_to_all | solution.py:26
  159.5 128.6 %all-to-all-start.2 = ((bf16[16,20,3072]{2,1,0:T(8,128)(2,1)}), bf16[16,20,3072]{2,1,0:T(8,128)(2,1)S(1)}, u32[]{:S(2)}, u32[]{:S(2)}) async-start(bf16[16,20,3072]{2,1,0:T(8,128)(2,1)} %stack.2), calls=%async_computation.2 | async-start | bytes 4718592 | tf_op jit(solution)/shard_map/all_to_all | solution.py:127
  166.8 135.0 %all-gather.6.cloned.1.call-start = ((), (), s32[]{:S(2)}) async-start(), calls=%async_computation.12 | async-start | bytes 2506752 | tf_op jit(solution)/shard_map/all_gather | solution.py:140
  288.0 28.3 %all-to-all-start.3 = ((bf16[32,256,96]{1,2,0:T(8,128)(2,1)}), bf16[32,256,96]{1,2,0:T(8,128)(2,1)}, u32[]{:S(2)}, u32[]{:S(2)}) async-start(bf16[32,256,96]{1,2,0:T(8,128)(2,1)} %bitcast.170), calls=%async_computation.3 | async-start | bytes 3145728 | tf_op jit(solution)/shard_map/all_to_all | solution.py:124
  293.9 107.7 %reduce-scatter.2.cloned.1.call-start = ((), (), s32[]{:S(2)}) async-start(), calls=%async_computation.11 | async-start | bytes 4177920 | tf_op jit(solution)/shard_map/reduce_scatter | solution.py:34
  336.0 66.8 %copy-start.4 = (bf16[32,20,96]{2,1,0:T(8,128)(2,1)S(1)}, bf16[32,20,96]{2,1,0:T(8,128)(2,1)}, u32[]{:S(2)}) copy-start(bf16[32,20,96]{2,1,0:T(8,128)(2,1)} %copy-done.3) | copy-start | bytes 368644
  336.7 85.7 %copy-start.43 = (f32[128]{0:T(128)S(1)}, f32[128]{0:T(128)}, u32[]{:S(2)}) copy-start(f32[128]{0:T(128)} %reduce_sum.89) | copy-start | bytes 1540
  404.1 26.6 %all-to-all-start.6 = ((bf16[20,32,98]{2,0,1:T(8,128)(2,1)}), bf16[20,32,98]{2,0,1:T(8,128)(2,1)S(1)}, u32[]{:S(2)}, u32[]{:S(2)}) async-start(bf16[20,32,98]{2,0,1:T(8,128)(2,1)} %copy.203), calls=%async_computation.7 | async-start | bytes 393216 | tf_op jit(solution)/shard_map/all_to_all | solution.py:162
  432.9 18.2 %all-to-all-start.7 = ((bf16[32,128,96]{1,2,0:T(8,128)(2,1)}), bf16[32,128,96]{1,2,0:T(8,128)(2,1)S(1)}, u32[]{:S(2)}, u32[]{:S(2)}) async-start(bf16[32,128,96]{1,2,0:T(8,128)(2,1)} %broadcast_in_dim.33), calls=%async_computation.8 | async-start | bytes 1572864 | tf_op jit(solution)/shard_map/all_to_all | solution.py:26
  453.6 48.0 %copy-start.6 = (f32[128,32,20]{0,1,2:T(8,128)S(1)}, f32[128,32,20]{0,1,2:T(8,128)}, u32[]{:S(2)}) copy-start(f32[128,32,20]{0,1,2:T(8,128)} %copy-done.5) | copy-start | bytes 983044
  454.9 46.6 %all-to-all-start.8 = ((bf16[20,32,96]{2,0,1:T(8,128)(2,1)}), bf16[20,32,96]{2,0,1:T(8,128)(2,1)S(1)}, u32[]{:S(2)}, u32[]{:S(2)}) async-start(bf16[20,32,96]{2,0,1:T(8,128)(2,1)} %copy.207), calls=%async_computation.9 | async-start | bytes 393216 | tf_op jit(solution)/shard_map/all_to_all | solution.py:183
  459.1 6.6 %collective-permute-start.4 = (f32[2,128,128]{2,1,0:T(8,128)S(1)}, f32[2,128,128]{2,1,0:T(8,128)S(1)}, u32[]{:S(2)}, u32[]{:S(2)}) collective-permute-start(f32[2,128,128]{2,1,0:T(8,128)S(1)} %convolution_bitcast_fusion.4), channel_id=1, source_target_pairs={{0,32},{32,0},{64,96},{96,64},{128,160},{160,128},{192,224},{224,1... | collective-permute-start | bytes 393224 | tf_op jit(solution)/shard_map/ppermute | solution.py:14
  461.7 57.0 %copy-start.21 = (bf16[128,256]{1,0:T(8,128)(2,1)S(1)}, bf16[128,256]{1,0:T(8,128)(2,1)}, u32[]{:S(2)}) copy-start(bf16[128,256]{1,0:T(8,128)(2,1)} %param.16) | copy-start | bytes 196612
  465.7 10.8 %collective-permute-start.5 = (f32[2,128,128]{2,1,0:T(8,128)S(1)}, f32[2,128,128]{2,1,0:T(8,128)S(1)}, u32[]{:S(2)}, u32[]{:S(2)}) collective-permute-start(f32[2,128,128]{2,1,0:T(8,128)S(1)} %add.138), channel_id=1, source_target_pairs={{0,64},{32,96},{64,0},{96,32},{128,192},{160,224},{192,128},{224,1... | collective-permute-start | bytes 393224 | tf_op jit(solution)/shard_map/ppermute | solution.py:14
  476.6 18.6 %collective-permute-start.6 = (f32[2,128,128]{2,1,0:T(8,128)S(1)}, f32[2,128,128]{2,1,0:T(8,128)S(1)}, u32[]{:S(2)}, u32[]{:S(2)}) collective-permute-start(f32[2,128,128]{2,1,0:T(8,128)S(1)} %add.140), channel_id=1, source_target_pairs={{0,128},{32,160},{64,192},{96,224},{128,0},{160,32},{192,64},{224,... | collective-permute-start | bytes 393224 | tf_op jit(solution)/shard_map/ppermute | solution.py:14
  495.2 21.8 %collective-permute-start.7 = (f32[2,128,128]{2,1,0:T(8,128)S(1)}, f32[2,128,128]{2,1,0:T(8,128)S(1)}, u32[]{:S(2)}, u32[]{:S(2)}) collective-permute-start(f32[2,128,128]{2,1,0:T(8,128)S(1)} %add.142), channel_id=1, source_target_pairs={{0,256},{32,288},{64,320},{96,352},{128,384},{160,416},{192,448},{... | collective-permute-start | bytes 393224 | tf_op jit(solution)/shard_map/ppermute | solution.py:14
  (33 other events, 521.2 us)
Sparse Core Ops, SparseCore 0:
  21.9 76.1 all-gather.3
  170.4 131.3 all-gather.5
  336.2 65.4 reduce-scatter.1
